TPU v7x, 32 devices: a whole 2x2x4 slice. The times are simulated.
32 devices in a mesh: clips: 2 (over y), rows: 4 (over z), tm: 2 (over x), chan: 2 (over core).
Axes of the slice: x: 2, y: 2, z: 4, core: 2. Of those that a mesh axis runs over, the one named last changes fastest.
Arguments:
- latent: bfloat16 [8, 4, 64, 512], P(('clips', 'tm'), 'rows', None, 'chan'), parts along dimension 0, may hold values from -24 to 24, as said below
- norm1_gain: float32 [512], P('chan'), may hold values from 0.5 to 1.5
- norm1_bias: float32 [512], P('chan'), may hold values from -1.2 to 1.2
- conv_weight: bfloat16 [13824, 512], P('rows', 'chan'), may hold values from -0.0546875 to 0.0546875
- conv_bias: float32 [512], P('chan'), may hold values from -1.2 to 1.2
- norm2_gain: float32 [512], P('chan'), may hold values from 0.5 to 1.5
- norm2_bias: float32 [512], P('chan'), may hold values from -1.2 to 1.2
- w_query: bfloat16 [512, 512], replicated, may hold values from -2 to 2
- b_query: float32 [512], replicated, may hold values from -1.2 to 1.2
- w_key: bfloat16 [512, 512], replicated, may hold values from -3 to 3
- w_value: bfloat16 [512, 512], replicated, may hold values from -0.25 to 0.25
- b_value: float32 [512], replicated, may hold values from -1.2 to 1.2
- w_out: bfloat16 [512, 512], replicated, may hold values from -0.25 to 0.25
- b_out: float32 [512], replicated, may hold values from -1.2 to 1.2
Outputs:
- decoded: bfloat16 [8, 4, 64, 512], P(('clips', 'tm'), 'rows', None, 'chan'), parts along dimension 0
There are 2 independent parts, one for each index of `clips`. A program takes and returns all parts, laid end to end along the dimension named above; an argument that names none is the same for every part. Nothing has to cross between parts.
Inputs may be any that keep to these rules, and one draw needn't show every extreme that they name: `latent`: activations of order one.
All inputs are finite; a program needn't handle non-finite values.
Results may differ from a plain program's by a relative error of at most 0.012.
The roundings to bfloat16 on the way count: a program that leaves them out, or rounds other values in their place, can miss the bound.
Values may be sent and summed in bfloat16 or wider, within the bound.
No kernel may reach another device: no remote copies, remote signals or barrier semaphores. Data moves between devices by JAX's collectives and lax.ppermute only.
A program may use at most 64 MiB of HBM per device.

v0:
```python
import jax
import jax.numpy as jnp
from jax import lax
from jax.sharding import PartitionSpec as P

C = 512
GROUPS = 32
EPSILON = 1e-06


def passed_along(value, axis, steps):
    count = lax.axis_size(axis)
    leading, last = (max(0, -steps), min(count, count - steps))
    return lax.ppermute(value, axis, [(source, source + steps) for source in range(leading, last)])


def with_halo(cells, sides, width):
    for axis, dim in sides:
        count = lax.axis_size(axis)
        ends = count - 1
        head = lax.slice_in_dim(cells, 0, width, axis=dim)
        tail = lax.slice_in_dim(cells, cells.shape[dim] - width, cells.shape[dim], axis=dim)
        cells = jnp.concatenate(
            [
                lax.ppermute(tail, axis, [(i, (i + 1) % count) for i in range(ends)]),
                cells,
                lax.ppermute(head, axis, [((i + 1) % count, i) for i in range(ends)]),
            ],
            axis=dim,
        )
    return cells


def group_view(values, group_size):
    full_shape = values.shape
    return values.astype(jnp.float32).reshape(
        full_shape[:-1] + (full_shape[-1] // group_size, group_size)
    )


def clip_normalize(latent, group_size):
    grouped = group_view(latent, group_size)
    cell_count = (
        grouped.shape[0]
        * grouped.shape[1]
        * grouped.shape[2]
        * group_size
        * lax.axis_size("rows")
        * lax.axis_size("tm")
    )
    group_mean = lax.psum(jnp.sum(grouped, axis=(0, 1, 2, 4)), ("rows", "tm")) / cell_count
    centered = grouped - group_mean[:, None]
    group_var = (
        lax.psum(jnp.sum(centered * centered, axis=(0, 1, 2, 4)), ("rows", "tm")) / cell_count
    )
    centered = grouped - group_mean[:, None]
    return (centered * lax.rsqrt(group_var + EPSILON)[:, None]).reshape(latent.shape)


def frame_normalize(middle, group_size):
    grouped = group_view(middle, group_size)
    cell_count = grouped.shape[1] * grouped.shape[2] * group_size * lax.axis_size("rows")
    group_mean = lax.psum(jnp.sum(grouped, axis=(1, 2, 4)), "rows") / cell_count
    centered = grouped - group_mean[:, None, None, :, None]
    group_var = lax.psum(jnp.sum(centered * centered, axis=(1, 2, 4)), "rows") / cell_count
    centered = grouped - group_mean[:, None, None, :, None]
    return (centered * lax.rsqrt(group_var + EPSILON)[:, None, None, :, None]).reshape(middle.shape)


def softmax_update(running, queries, key_block, value_block, score_scale):
    row_peak, weight_sum, accumulated = running
    scores = (
        jnp.einsum("fqc,fkc->fqk", queries, key_block, preferred_element_type=jnp.float32)
        * score_scale
    )
    new_peak = jnp.max(scores, axis=2)
    factor = jnp.exp(row_peak - new_peak)
    weights = jnp.exp(scores - new_peak[:, :, None])
    weight_sum = weight_sum * factor + jnp.sum(weights, axis=2)
    accumulated = accumulated * factor[:, :, None] + jnp.einsum(
        "fqk,fkc->fqc",
        weights.astype(jnp.bfloat16),
        value_block,
        preferred_element_type=jnp.float32,
    )
    return (new_peak, weight_sum, accumulated)


def local(
    latent,
    norm1_gain,
    norm1_bias,
    conv_weight,
    conv_bias,
    norm2_gain,
    norm2_bias,
    w_query,
    b_query,
    w_key,
    w_value,
    b_value,
    w_out,
    b_out,
):
    frames, rows_here, columns, channels = latent.shape
    group_size = C // GROUPS
    activated = jax.nn.silu(clip_normalize(latent, group_size) * norm1_gain + norm1_bias).astype(
        jnp.bfloat16
    )
    all_channels = lax.all_gather(activated, "chan", axis=3, tiled=True)
    carried = passed_along(all_channels, "tm", 1)
    carried = jnp.where(
        lax.axis_index("tm") == 0, jnp.broadcast_to(all_channels[:1], carried.shape), carried
    )
    timed = jnp.concatenate([carried, all_channels], axis=0)
    rimmed = with_halo(timed, (("rows", 1),), 1)
    row_place = lax.axis_index("rows")
    upper_rim = jnp.where(row_place == 0, rimmed[:, 1:2], rimmed[:, :1])
    lower_rim = jnp.where(row_place == lax.axis_size("rows") - 1, rimmed[:, -2:-1], rimmed[:, -1:])
    rimmed = jnp.concatenate([upper_rim, rimmed[:, 1:-1], lower_rim], axis=1)
    padded = jnp.concatenate([rimmed[:, :, :1], rimmed, rimmed[:, :, -1:]], axis=2)
    windows = []
    for frame_step in range(3):
        for row_step in range(3):
            for column_step in range(3):
                windows.append(
                    padded[
                        frame_step : frame_step + frames,
                        row_step : row_step + rows_here,
                        column_step : column_step + columns,
                    ].reshape(-1, C)
                )
    patches = jnp.concatenate(windows, axis=1)
    convolved = jnp.dot(
        patches,
        lax.all_gather(conv_weight, "rows", axis=0, tiled=True),
        preferred_element_type=jnp.float32,
    )
    middle = (latent.astype(jnp.float32) + (convolved + conv_bias).reshape(latent.shape)).astype(
        jnp.bfloat16
    )
    normed = (frame_normalize(middle, group_size) * norm2_gain + norm2_bias).astype(jnp.bfloat16)
    swapped = lax.all_to_all(normed, "chan", split_axis=0, concat_axis=3, tiled=True)
    frame_count = swapped.shape[0]
    local_tokens = rows_here * columns
    flattened = swapped.reshape(-1, C)
    queries = (
        (jnp.dot(flattened, w_query, preferred_element_type=jnp.float32) + b_query)
        .astype(jnp.bfloat16)
        .reshape(frame_count, local_tokens, C)
    )
    score_scale = C ** (-0.5)
    initial = (
        jnp.full((frame_count, local_tokens), -jnp.inf, jnp.float32),
        jnp.zeros((frame_count, local_tokens), jnp.float32),
        jnp.zeros((frame_count, local_tokens, C), jnp.float32),
    )
    feature_rows = swapped.reshape(frame_count, local_tokens, C)
    shard_flat = lax.all_gather(feature_rows, "rows", axis=1, tiled=True).reshape(-1, C)
    key_block = (
        jnp.dot(shard_flat, w_key, preferred_element_type=jnp.float32)
        .astype(jnp.bfloat16)
        .reshape(frame_count, -1, C)
    )
    value_block = (
        (jnp.dot(shard_flat, w_value, preferred_element_type=jnp.float32) + b_value)
        .astype(jnp.bfloat16)
        .reshape(frame_count, -1, C)
    )
    row_peak, weight_sum, accumulated = softmax_update(
        initial, queries, key_block, value_block, score_scale
    )
    attended = (accumulated / weight_sum[:, :, None]).astype(jnp.bfloat16)
    branch = (
        (jnp.dot(attended.reshape(-1, C), w_out, preferred_element_type=jnp.float32) + b_out)
        .astype(jnp.bfloat16)
        .reshape(frame_count, rows_here, columns, C)
    )
    returned = lax.all_to_all(branch, "chan", split_axis=3, concat_axis=0, tiled=True)
    return (middle.astype(jnp.float32) + returned.astype(jnp.float32)).astype(jnp.bfloat16)


def solution(mesh):
    in_specs = (
        P(("clips", "tm"), "rows", None, "chan"),
        P("chan"),
        P("chan"),
        P("rows", "chan"),
        P("chan"),
        P("chan"),
        P("chan"),
        P(),
        P(),
        P(),
        P(),
        P(),
        P(),
        P(),
    )
    out_specs = P(("clips", "tm"), "rows", None, "chan")
    return jax.shard_map(local, mesh=mesh, in_specs=in_specs, out_specs=out_specs, check_vma=False)
```

profile of v0, /device:TPU:0, one launch (start us, length us, event | category | flops | bytes accessed | tf_op | source)
XLA Modules:
  0.0 204.5 jit_solution(6646806189756094243)
XLA Ops:
  6.5 0.7 all-gather.2.cloned.1.call-update
  7.3 0.9 convert_reduce_fusion.1
  8.3 23.4 %psum.28 = f32[16]{0:T(128)S(1)} all-reduce(f32[16]{0:T(128)S(1)} %reduce_sum.59), channel_id=1, replica_groups=mesh['clips'=2,'rows'=4,'tm'=2,'chan'=2] {'rows','tm'}, use_global_device_ids=true, to_apply=%region_2.0 | all-reduce | flops 16 | bytes 128 | tf_op jit(solution)/shard_map/psum | solution.py:51
  31.9 0.9 fusion.39
  33.0 17.6 %psum.29 = f32[16]{0:T(128)S(1)} all-reduce(f32[16]{0:T(128)S(1)} %reduce_sum.62), channel_id=1, replica_groups=mesh['clips'=2,'rows'=4,'tm'=2,'chan'=2] {'rows','tm'}, use_global_device_ids=true, to_apply=%region_5.6 | all-reduce | flops 16 | bytes 128 | tf_op jit(solution)/shard_map/psum | solution.py:54
  50.8 0.9 fusion.47
  51.7 1.9 all_gather.9
  53.6 3.9 %collective-permute-start = (bf16[2,1,64,512]{3,2,1,0:T(8,128)(2,1)S(1)}, bf16[2,1,64,512]{3,2,1,0:T(8,128)(2,1)S(1)}, u32[]{:S(2)}, u32[]{:S(2)}) collective-permute-start(bf16[2,1,64,512]{3,2,1,0:T(8,128)(2,1)S(1)} %all_gather.9), channel_id=1, source_target_pairs={{0,2},{1,3},{4,6},{5,7},{8,10},{9,11},{12,14},{13,15},{16,18},{17,... | collective-permute-start | bytes 393224 | tf_op jit(solution)/shard_map/ppermute | solution.py:14
  57.5 3.0 %collective-permute-done = bf16[2,1,64,512]{3,2,1,0:T(8,128)(2,1)S(1)} collective-permute-done((bf16[2,1,64,512]{3,2,1,0:T(8,128)(2,1)S(1)}, bf16[2,1,64,512]{3,2,1,0:T(8,128)(2,1)S(1)}, u32[]{:S(2)}, u32[]{:S(2)}) %collective-permute-start) | collective-permute-done | bytes 131104 | tf_op jit(solution)/shard_map/ppermute | solution.py:14
  60.6 2.1 %collective-permute-start.1 = (bf16[4,1,64,512]{3,2,1,0:T(8,128)(2,1)S(1)}, bf16[4,1,64,512]{3,2,1,0:T(8,128)(2,1)S(1)}, u32[]{:S(2)}, u32[]{:S(2)}) collective-permute-start(bf16[4,1,64,512]{3,2,1,0:T(8,128)(2,1)S(1)} %pad_maximum_fusion.6), channel_id=1, source_target_pairs={{0,4},{4,8},{8,12},{1,5},{5,9},{9,13},{2,6},{6,10},{10,14},{3,7},{... | collective-permute-start | bytes 786440 | tf_op jit(solution)/shard_map/ppermute | solution.py:25
  62.7 1.3 collective-permute-start.2
  64.1 10.4 %collective-permute-done.1 = bf16[4,1,64,512]{3,2,1,0:T(8,128)(2,1)S(1)} collective-permute-done((bf16[4,1,64,512]{3,2,1,0:T(8,128)(2,1)S(1)}, bf16[4,1,64,512]{3,2,1,0:T(8,128)(2,1)S(1)}, u32[]{:S(2)}, u32[]{:S(2)}) %collective-permute-start.1) | collective-permute-done | bytes 262176 | tf_op jit(solution)/shard_map/ppermute | solution.py:25
  74.4 9.7 %collective-permute-done.2 = bf16[4,1,64,512]{3,2,1,0:T(8,128)(2,1)S(1)} collective-permute-done((bf16[4,1,64,512]{3,2,1,0:T(8,128)(2,1)S(1)}, bf16[4,1,64,512]{3,2,1,0:T(8,128)(2,1)S(1)}, u32[]{:S(2)}, u32[]{:S(2)}) %collective-permute-start.2) | collective-permute-done | bytes 262176 | tf_op jit(solution)/shard_map/ppermute | solution.py:27
  85.0 0.7 constant_dynamic-update-slice_fusion.26
  96.0 0.7 constant_dynamic-update-slice_fusion.10
  98.8 0.7 constant_dynamic-update-slice_fusion.6
  103.6 42.1 %all-gather.2.cloned.1.call-done = bf16[13824,256]{1,0:T(8,128)(2,1)} async-done(((bf16[3456,256]{1,0:T(8,128)(2,1)}), bf16[13824,256]{1,0:T(8,128)(2,1)}) %all-gather.2.cloned.1.call-update) | async-done | bytes 7077904 | tf_op jit(solution)/shard_map/all_gather | solution.py:136
  145.7 5.2 %convert_reduce_fusion = (f32[2,256]{1,0:T(2,128)S(1)}, bf16[2,1,64,256]{3,2,1,0:T(8,128)(2,1)S(1)}) fusion(bf16[2,1,64,256]{3,2,1,0:T(8,128)(2,1)S(1)} %copy-done.1, f32[256]{0:T(256)S(1)} %copy-done.5, bf16[13824,256]{1,0:T(8,128)(2,1)} %all-gather.2.cloned.1.call-done, bf16[128,13824]{1,0:T(8,128)(2,1)} %constant_dynamic-update-slice_fusion), kind=kOutput, calls=%fused_computation.49 | convolution fusion | flops 906165760 | bytes 10750976 | tf_op jit(solution)/shard_map/dot_general | solution.py:134
  151.1 8.7 %psum.30 = f32[2,16]{1,0:T(2,128)S(1)} all-reduce(f32[2,16]{1,0:T(2,128)S(1)} %reduce_sum.81), channel_id=1, replica_groups=mesh['clips'=2,'rows'=4,'tm'=2,'chan'=2] {'rows'}, use_global_device_ids=true, to_apply=%region_8.9 | all-reduce | flops 32 | bytes 256 | tf_op jit(solution)/shard_map/psum | solution.py:63
  160.1 10.1 %psum.31 = f32[2,16]{1,0:T(2,128)S(1)} all-reduce(f32[2,16]{1,0:T(2,128)S(1)} %reduce_sum.84), channel_id=1, replica_groups=mesh['clips'=2,'rows'=4,'tm'=2,'chan'=2] {'rows'}, use_global_device_ids=true, to_apply=%region_11.12 | all-reduce | flops 32 | bytes 256 | tf_op jit(solution)/shard_map/psum | solution.py:65
  170.4 3.8 %all_to_all.24 = bf16[2,1,64,256]{3,2,1,0:T(8,128)(2,1)S(1)} all-to-all(bf16[2,1,64,256]{3,2,1,0:T(8,128)(2,1)S(1)} %fusion.38), channel_id=1, replica_groups=mesh['clips'=2,'rows'=4,'tm'=2,'chan'=2] {'chan'}, dimensions={0} | all-to-all | bytes 131072 | tf_op jit(solution)/shard_map/all_to_all | solution.py:143
  174.3 14.3 %all_gather.11 = bf16[1,256,512]{2,1,0:T(8,128)(2,1)S(1)} all-gather(bf16[1,64,512]{2,1,0:T(8,128)(2,1)S(1)} %reshape.270), channel_id=1, replica_groups=mesh['clips'=2,'rows'=4,'tm'=2,'chan'=2] {'rows'}, dimensions={1}, use_global_device_ids=true | all-gather | bytes 327680 | tf_op jit(solution)/shard_map/all_gather | solution.py:159
  191.0 1.4 reduce.14
  192.6 3.8 %all_to_all.25 = bf16[2,2,8192]{2,1,0:T(2,128)(2,1)S(1)} all-to-all(bf16[2,2,8192]{2,1,0:T(2,128)(2,1)S(1)} %reshape.275), channel_id=1, replica_groups=mesh['clips'=2,'rows'=4,'tm'=2,'chan'=2] {'chan'}, dimensions={0} | all-to-all | bytes 131072 | tf_op jit(solution)/shard_map/all_to_all | solution.py:179
  (93 shorter events, 22.5 us)
Async XLA Ops:
  6.5 182.1 %copy-start = (bf16[512,512]{1,0:T(8,128)(2,1)S(1)}, bf16[512,512]{1,0:T(8,128)(2,1)}, u32[]{:S(2)}) copy-start(bf16[512,512]{1,0:T(8,128)(2,1)} %param.21) | copy-start | bytes 1572868
  6.5 139.1 %all-gather.2.cloned.1.call-start = ((), (), s32[]{:S(2)}) async-start(), calls=%async_computation.2 | async-start | bytes 8847360 | tf_op jit(solution)/shard_map/all_gather | solution.py:136
  53.6 6.9 %collective-permute-start = (bf16[2,1,64,512]{3,2,1,0:T(8,128)(2,1)S(1)}, bf16[2,1,64,512]{3,2,1,0:T(8,128)(2,1)S(1)}, u32[]{:S(2)}, u32[]{:S(2)}) collective-permute-start(bf16[2,1,64,512]{3,2,1,0:T(8,128)(2,1)S(1)} %all_gather.9), channel_id=1, source_target_pairs={{0,2},{1,3},{4,6},{5,7},{8,10},{9,11},{12,14},{13,15},{16,18},{17,... | collective-permute-start | bytes 393224 | tf_op jit(solution)/shard_map/ppermute | solution.py:14
  60.6 13.8 %collective-permute-start.1 = (bf16[4,1,64,512]{3,2,1,0:T(8,128)(2,1)S(1)}, bf16[4,1,64,512]{3,2,1,0:T(8,128)(2,1)S(1)}, u32[]{:S(2)}, u32[]{:S(2)}) collective-permute-start(bf16[4,1,64,512]{3,2,1,0:T(8,128)(2,1)S(1)} %pad_maximum_fusion.6), channel_id=1, source_target_pairs={{0,4},{4,8},{8,12},{1,5},{5,9},{9,13},{2,6},{6,10},{10,14},{3,7},{... | collective-permute-start | bytes 786440 | tf_op jit(solution)/shard_map/ppermute | solution.py:25
  62.7 21.4 %collective-permute-start.2 = (bf16[4,1,64,512]{3,2,1,0:T(8,128)(2,1)S(1)}, bf16[4,1,64,512]{3,2,1,0:T(8,128)(2,1)S(1)}, u32[]{:S(2)}, u32[]{:S(2)}) collective-permute-start(bf16[4,1,64,512]{3,2,1,0:T(8,128)(2,1)S(1)} %pad_maximum_fusion.6), channel_id=1, source_target_pairs={{4,0},{8,4},{12,8},{5,1},{9,5},{13,9},{6,2},{10,6},{14,10},{7,3},{... | collective-permute-start | bytes 786440 | tf_op jit(solution)/shard_map/ppermute | solution.py:27
  85.8 59.9 %copy-start.1 = (bf16[2,1,64,256]{3,2,1,0:T(8,128)(2,1)S(1)}, bf16[2,1,64,256]{3,2,1,0:T(8,128)(2,1)}, u32[]{:S(2)}) copy-start(bf16[2,1,64,256]{3,2,1,0:T(8,128)(2,1)} %param.14) | copy-start | bytes 196612
  85.8 59.9 %copy-start.5 = (f32[256]{0:T(256)S(1)}, f32[256]{0:T(256)}, u32[]{:S(2)}) copy-start(f32[256]{0:T(256)} %param.18) | copy-start | bytes 3076
  103.6 66.8 %copy-start.6 = (f32[256]{0:T(256)S(1)}, f32[256]{0:T(256)}, u32[]{:S(2)}) copy-start(f32[256]{0:T(256)} %param.20) | copy-start | bytes 3076
  103.6 66.8 %copy-start.7 = (f32[256]{0:T(256)S(1)}, f32[256]{0:T(256)}, u32[]{:S(2)}) copy-start(f32[256]{0:T(256)} %param.19) | copy-start | bytes 3076
  103.6 85.1 %copy-start.3 = (f32[512]{0:T(512)S(1)}, f32[512]{0:T(512)}, u32[]{:S(2)}) copy-start(f32[512]{0:T(512)} %param.22) | copy-start | bytes 6148
  103.6 85.3 %copy-start.8 = (bf16[512,512]{1,0:T(8,128)(2,1)S(1)}, bf16[512,512]{1,0:T(8,128)(2,1)}, u32[]{:S(2)}) copy-start(bf16[512,512]{1,0:T(8,128)(2,1)} %param.23) | copy-start | bytes 1572868
  103.6 86.1 %copy-start.9 = (bf16[512,512]{1,0:T(8,128)(2,1)S(1)}, bf16[512,512]{1,0:T(8,128)(2,1)}, u32[]{:S(2)}) copy-start(bf16[512,512]{1,0:T(8,128)(2,1)} %param.24) | copy-start | bytes 1572868
  103.6 86.1 %copy-start.10 = (f32[512]{0:T(512)S(1)}, f32[512]{0:T(512)}, u32[]{:S(2)}) copy-start(f32[512]{0:T(512)} %param.25) | copy-start | bytes 6148
  150.9 39.3 %copy-start.2 = (bf16[512,512]{1,0:T(8,128)(2,1)S(1)}, bf16[512,512]{1,0:T(8,128)(2,1)}, u32[]{:S(2)}) copy-start(bf16[512,512]{1,0:T(8,128)(2,1)} %param.26) | copy-start | bytes 1572868
  150.9 39.3 %copy-start.4 = (f32[512]{0:T(512)S(1)}, f32[512]{0:T(512)}, u32[]{:S(2)}) copy-start(f32[512]{0:T(512)} %param.27) | copy-start | bytes 6148
Sparse Core Ops, SparseCore 0:
  8.9 136.6 all-gather.1
where the time goes:
time: 205 us; the launch traced here: 204 us
  blocking collectives  83.6 us (41%)
  waiting for transfers between devices  65.9 us (32%)
  local copies, waits for them, and re-layouts  21.1 us (10%)
  between operations  13.7 us (7%)
  starting transfers between devices  7.29 us (4%)
  matrix products  6.57 us (3%)
  other arithmetic  6.28 us (3%)
    all_gather x1, waiting for transfers between devices, local(): lax.all_gather(conv_weight, 'rows', axis=0, tiled=True)  42.1 us
    psum x1, blocking collectives, clip_normalize(): lax.psum(jnp.sum(grouped, axis=(0, 1, 2, 4)), ('rows', 'tm')) / cell_count  23.4 us
    unnamed x52, local copies, waits for them, and re-layouts  18.7 us
    psum x1, blocking collectives, clip_normalize(): lax.psum(jnp.sum(centered * centered, axis=(0, 1, 2, 4)), ('rows', 'tm'))  17.6 us
    all_gather x1, blocking collectives, local(): lax.all_gather(feature_rows, 'rows', axis=1, tiled=True).reshape(-1, C)  14.3 us
    ppermute x1, waiting for transfers between devices, with_halo(): lax.ppermute(tail, axis, [(i, (i + 1) % count) for i in range(ends)])  10.4 us
    psum x1, blocking collectives, frame_normalize(): lax.psum(jnp.sum(centered * centered, axis=(1, 2, 4)), 'rows') / cell_count  10.1 us
    ppermute x1, waiting for transfers between devices, with_halo(): lax.ppermute(head, axis, [((i + 1) % count, i) for i in range(ends)])  9.72 us
  transfers between devices with their start and end apart: 4, of which 4 were waited for; matrix products, arithmetic and copies ran while one was open for 11% of the time, Pallas kernels for 0%

commit v1 on v0

--- a/solution.py
+++ b/solution.py
@@ -51,7 +51,8 @@
     group_mean = lax.psum(jnp.sum(grouped, axis=(0, 1, 2, 4)), ("rows", "tm")) / cell_count
     centered = grouped - group_mean[:, None]
     group_var = (
-        lax.psum(jnp.sum(centered * centered, axis=(0, 1, 2, 4)), ("rows", "tm")) / cell_count
+        lax.psum(lax.psum(jnp.sum(centered * centered, axis=(0, 1, 2, 4)), "tm"), "rows")
+        / cell_count
     )
     centered = grouped - group_mean[:, None]
     return (centered * lax.rsqrt(group_var + EPSILON)[:, None]).reshape(latent.shape)

time: 205 us -> 205 us (level)
  blocking collectives: 83.6 us -> 79.8 us
  waiting for transfers between devices: 65.9 us -> 68.8 us
    psum x1 -> x2, blocking collectives: 17.6 us -> 13.9 us  [the longest x1 8.94 us: clip_normalize(): lax.psum(lax.psum(jnp.sum(centered * centered, axis=(0, 1, 2, 4)), 'tm'),...]
where the time goes in v1:
time: 205 us; the launch traced here: 204 us
  blocking collectives  79.8 us (39%)
  waiting for transfers between devices  68.8 us (34%)
  local copies, waits for them, and re-layouts  21.1 us (10%)
  between operations  13.7 us (7%)
  starting transfers between devices  8.13 us (4%)
  matrix products  6.57 us (3%)
  other arithmetic  6.28 us (3%)
    all_gather x1, waiting for transfers between devices, local(): lax.all_gather(conv_weight, 'rows', axis=0, tiled=True)  43.8 us
    psum x1, blocking collectives, clip_normalize(): lax.psum(jnp.sum(grouped, axis=(0, 1, 2, 4)), ('rows', 'tm')) / cell_count  23.4 us
    unnamed x52, local copies, waits for them, and re-layouts  18.7 us
    all_gather x1, blocking collectives, local(): lax.all_gather(feature_rows, 'rows', axis=1, tiled=True).reshape(-1, C)  14.3 us
    ppermute x1, waiting for transfers between devices, with_halo(): lax.ppermute(head, axis, [((i + 1) % count, i) for i in range(ends)])  10.8 us
    ppermute x1, waiting for transfers between devices, with_halo(): lax.ppermute(tail, axis, [(i, (i + 1) % count) for i in range(ends)])  10.4 us
    psum x1, blocking collectives, frame_normalize(): lax.psum(jnp.sum(centered * centered, axis=(1, 2, 4)), 'rows') / cell_count  10 us
    psum x1, blocking collectives, clip_normalize(): lax.psum(lax.psum(jnp.sum(centered * centered, axis=(0, 1, 2, 4)), 'tm'),...  8.94 us
  transfers between devices with their start and end apart: 4, of which 4 were waited for; matrix products, arithmetic and copies ran while one was open for 11% of the time, Pallas kernels for 0%

profile of v1, /device:TPU:0, one launch (start us, length us, event | category | flops | bytes accessed | tf_op | source)
XLA Modules:
  0.0 204.4 jit_solution(12584682356806645970)
XLA Ops:
  6.5 0.7 all-gather.2.cloned.1.call-update
  7.3 0.9 convert_reduce_fusion.1
  8.3 23.4 %psum.35 = f32[16]{0:T(128)S(1)} all-reduce(f32[16]{0:T(128)S(1)} %reduce_sum.59), channel_id=1, replica_groups=mesh['clips'=2,'rows'=4,'tm'=2,'chan'=2] {'rows','tm'}, use_global_device_ids=true, to_apply=%region_2.0 | all-reduce | flops 16 | bytes 128 | tf_op jit(solution)/shard_map/psum | solution.py:51
  31.9 0.9 fusion.39
  33.0 4.9 %psum.36 = f32[16]{0:T(128)S(1)} all-reduce(f32[16]{0:T(128)S(1)} %reduce_sum.62), channel_id=1, replica_groups=mesh['clips'=2,'rows'=4,'tm'=2,'chan'=2] {'tm'}, use_global_device_ids=true, to_apply=%region_5.6 | all-reduce | flops 16 | bytes 128 | tf_op jit(solution)/shard_map/psum | solution.py:54
  37.9 8.9 %psum.37 = f32[16]{0:T(128)S(1)} all-reduce(f32[16]{0:T(128)S(1)} %psum.36), channel_id=1, replica_groups=mesh['clips'=2,'rows'=4,'tm'=2,'chan'=2] {'rows'}, use_global_device_ids=true, to_apply=%region_6.7 | all-reduce | flops 16 | bytes 128 | tf_op jit(solution)/shard_map/psum | solution.py:54
  47.0 0.9 fusion.47
  48.0 1.9 all_gather.9
  49.9 3.4 %collective-permute-start = (bf16[2,1,64,512]{3,2,1,0:T(8,128)(2,1)S(1)}, bf16[2,1,64,512]{3,2,1,0:T(8,128)(2,1)S(1)}, u32[]{:S(2)}, u32[]{:S(2)}) collective-permute-start(bf16[2,1,64,512]{3,2,1,0:T(8,128)(2,1)S(1)} %all_gather.9), channel_id=1, source_target_pairs={{0,2},{1,3},{4,6},{5,7},{8,10},{9,11},{12,14},{13,15},{16,18},{17,... | collective-permute-start | bytes 393224 | tf_op jit(solution)/shard_map/ppermute | solution.py:14
  53.3 3.0 %collective-permute-done = bf16[2,1,64,512]{3,2,1,0:T(8,128)(2,1)S(1)} collective-permute-done((bf16[2,1,64,512]{3,2,1,0:T(8,128)(2,1)S(1)}, bf16[2,1,64,512]{3,2,1,0:T(8,128)(2,1)S(1)}, u32[]{:S(2)}, u32[]{:S(2)}) %collective-permute-start) | collective-permute-done | bytes 131104 | tf_op jit(solution)/shard_map/ppermute | solution.py:14
  56.4 3.4 %collective-permute-start.1 = (bf16[4,1,64,512]{3,2,1,0:T(8,128)(2,1)S(1)}, bf16[4,1,64,512]{3,2,1,0:T(8,128)(2,1)S(1)}, u32[]{:S(2)}, u32[]{:S(2)}) collective-permute-start(bf16[4,1,64,512]{3,2,1,0:T(8,128)(2,1)S(1)} %pad_maximum_fusion.6), channel_id=1, source_target_pairs={{0,4},{4,8},{8,12},{1,5},{5,9},{9,13},{2,6},{6,10},{10,14},{3,7},{... | collective-permute-start | bytes 786440 | tf_op jit(solution)/shard_map/ppermute | solution.py:25
  59.8 1.3 collective-permute-start.2
  61.1 10.4 %collective-permute-done.1 = bf16[4,1,64,512]{3,2,1,0:T(8,128)(2,1)S(1)} collective-permute-done((bf16[4,1,64,512]{3,2,1,0:T(8,128)(2,1)S(1)}, bf16[4,1,64,512]{3,2,1,0:T(8,128)(2,1)S(1)}, u32[]{:S(2)}, u32[]{:S(2)}) %collective-permute-start.1) | collective-permute-done | bytes 262176 | tf_op jit(solution)/shard_map/ppermute | solution.py:25
  71.5 10.8 %collective-permute-done.2 = bf16[4,1,64,512]{3,2,1,0:T(8,128)(2,1)S(1)} collective-permute-done((bf16[4,1,64,512]{3,2,1,0:T(8,128)(2,1)S(1)}, bf16[4,1,64,512]{3,2,1,0:T(8,128)(2,1)S(1)}, u32[]{:S(2)}, u32[]{:S(2)}) %collective-permute-start.2) | collective-permute-done | bytes 262176 | tf_op jit(solution)/shard_map/ppermute | solution.py:27
  83.2 0.7 constant_dynamic-update-slice_fusion.26
  97.0 0.7 constant_dynamic-update-slice_fusion.6
  101.8 43.8 %all-gather.2.cloned.1.call-done = bf16[13824,256]{1,0:T(8,128)(2,1)} async-done(((bf16[3456,256]{1,0:T(8,128)(2,1)}), bf16[13824,256]{1,0:T(8,128)(2,1)}) %all-gather.2.cloned.1.call-update) | async-done | bytes 7077904 | tf_op jit(solution)/shard_map/all_gather | solution.py:137
  145.6 5.2 %convert_reduce_fusion = (f32[2,256]{1,0:T(2,128)S(1)}, bf16[2,1,64,256]{3,2,1,0:T(8,128)(2,1)S(1)}) fusion(bf16[2,1,64,256]{3,2,1,0:T(8,128)(2,1)S(1)} %copy-done.1, f32[256]{0:T(256)S(1)} %copy-done.5, bf16[13824,256]{1,0:T(8,128)(2,1)} %all-gather.2.cloned.1.call-done, bf16[128,13824]{1,0:T(8,128)(2,1)} %constant_dynamic-update-slice_fusion), kind=kOutput, calls=%fused_computation.49 | convolution fusion | flops 906165760 | bytes 10750976 | tf_op jit(solution)/shard_map/dot_general | solution.py:135
  151.0 8.7 %psum.38 = f32[2,16]{1,0:T(2,128)S(1)} all-reduce(f32[2,16]{1,0:T(2,128)S(1)} %reduce_sum.81), channel_id=1, replica_groups=mesh['clips'=2,'rows'=4,'tm'=2,'chan'=2] {'rows'}, use_global_device_ids=true, to_apply=%region_9.10 | all-reduce | flops 32 | bytes 256 | tf_op jit(solution)/shard_map/psum | solution.py:64
  160.1 10.0 %psum.39 = f32[2,16]{1,0:T(2,128)S(1)} all-reduce(f32[2,16]{1,0:T(2,128)S(1)} %reduce_sum.84), channel_id=1, replica_groups=mesh['clips'=2,'rows'=4,'tm'=2,'chan'=2] {'rows'}, use_global_device_ids=true, to_apply=%region_12.13 | all-reduce | flops 32 | bytes 256 | tf_op jit(solution)/shard_map/psum | solution.py:66
  170.4 3.8 %all_to_all.24 = bf16[2,1,64,256]{3,2,1,0:T(8,128)(2,1)S(1)} all-to-all(bf16[2,1,64,256]{3,2,1,0:T(8,128)(2,1)S(1)} %fusion.38), channel_id=1, replica_groups=mesh['clips'=2,'rows'=4,'tm'=2,'chan'=2] {'chan'}, dimensions={0} | all-to-all | bytes 131072 | tf_op jit(solution)/shard_map/all_to_all | solution.py:144
  174.3 14.3 %all_gather.11 = bf16[1,256,512]{2,1,0:T(8,128)(2,1)S(1)} all-gather(bf16[1,64,512]{2,1,0:T(8,128)(2,1)S(1)} %reshape.270), channel_id=1, replica_groups=mesh['clips'=2,'rows'=4,'tm'=2,'chan'=2] {'rows'}, dimensions={1}, use_global_device_ids=true | all-gather | bytes 327680 | tf_op jit(solution)/shard_map/all_gather | solution.py:160
  191.0 1.4 reduce.14
  192.6 3.8 %all_to_all.25 = bf16[2,2,8192]{2,1,0:T(2,128)(2,1)S(1)} all-to-all(bf16[2,2,8192]{2,1,0:T(2,128)(2,1)S(1)} %reshape.275), channel_id=1, replica_groups=mesh['clips'=2,'rows'=4,'tm'=2,'chan'=2] {'chan'}, dimensions={0} | all-to-all | bytes 131072 | tf_op jit(solution)/shard_map/all_to_all | solution.py:180
  (94 shorter events, 23.2 us)
Async XLA Ops:
  6.5 182.1 %copy-start = (bf16[512,512]{1,0:T(8,128)(2,1)S(1)}, bf16[512,512]{1,0:T(8,128)(2,1)}, u32[]{:S(2)}) copy-start(bf16[512,512]{1,0:T(8,128)(2,1)} %param.21) | copy-start | bytes 1572868
  6.5 139.1 %all-gather.2.cloned.1.call-start = ((), (), s32[]{:S(2)}) async-start(), calls=%async_computation.2 | async-start | bytes 8847360 | tf_op jit(solution)/shard_map/all_gather | solution.py:137
  49.9 6.5 %collective-permute-start = (bf16[2,1,64,512]{3,2,1,0:T(8,128)(2,1)S(1)}, bf16[2,1,64,512]{3,2,1,0:T(8,128)(2,1)S(1)}, u32[]{:S(2)}, u32[]{:S(2)}) collective-permute-start(bf16[2,1,64,512]{3,2,1,0:T(8,128)(2,1)S(1)} %all_gather.9), channel_id=1, source_target_pairs={{0,2},{1,3},{4,6},{5,7},{8,10},{9,11},{12,14},{13,15},{16,18},{17,... | collective-permute-start | bytes 393224 | tf_op jit(solution)/shard_map/ppermute | solution.py:14
  56.4 15.1 %collective-permute-start.1 = (bf16[4,1,64,512]{3,2,1,0:T(8,128)(2,1)S(1)}, bf16[4,1,64,512]{3,2,1,0:T(8,128)(2,1)S(1)}, u32[]{:S(2)}, u32[]{:S(2)}) collective-permute-start(bf16[4,1,64,512]{3,2,1,0:T(8,128)(2,1)S(1)} %pad_maximum_fusion.6), channel_id=1, source_target_pairs={{0,4},{4,8},{8,12},{1,5},{5,9},{9,13},{2,6},{6,10},{10,14},{3,7},{... | collective-permute-start | bytes 786440 | tf_op jit(solution)/shard_map/ppermute | solution.py:25
  59.8 22.5 %collective-permute-start.2 = (bf16[4,1,64,512]{3,2,1,0:T(8,128)(2,1)S(1)}, bf16[4,1,64,512]{3,2,1,0:T(8,128)(2,1)S(1)}, u32[]{:S(2)}, u32[]{:S(2)}) collective-permute-start(bf16[4,1,64,512]{3,2,1,0:T(8,128)(2,1)S(1)} %pad_maximum_fusion.6), channel_id=1, source_target_pairs={{4,0},{8,4},{12,8},{5,1},{9,5},{13,9},{6,2},{10,6},{14,10},{7,3},{... | collective-permute-start | bytes 786440 | tf_op jit(solution)/shard_map/ppermute | solution.py:27
  84.0 61.7 %copy-start.1 = (bf16[2,1,64,256]{3,2,1,0:T(8,128)(2,1)S(1)}, bf16[2,1,64,256]{3,2,1,0:T(8,128)(2,1)}, u32[]{:S(2)}) copy-start(bf16[2,1,64,256]{3,2,1,0:T(8,128)(2,1)} %param.14) | copy-start | bytes 196612
  84.0 61.6 %copy-start.5 = (f32[256]{0:T(256)S(1)}, f32[256]{0:T(256)}, u32[]{:S(2)}) copy-start(f32[256]{0:T(256)} %param.18) | copy-start | bytes 3076
  101.8 68.5 %copy-start.6 = (f32[256]{0:T(256)S(1)}, f32[256]{0:T(256)}, u32[]{:S(2)}) copy-start(f32[256]{0:T(256)} %param.20) | copy-start | bytes 3076
  101.8 68.5 %copy-start.7 = (f32[256]{0:T(256)S(1)}, f32[256]{0:T(256)}, u32[]{:S(2)}) copy-start(f32[256]{0:T(256)} %param.19) | copy-start | bytes 3076
  101.8 86.8 %copy-start.3 = (f32[512]{0:T(512)S(1)}, f32[512]{0:T(512)}, u32[]{:S(2)}) copy-start(f32[512]{0:T(512)} %param.22) | copy-start | bytes 6148
  101.8 87.1 %copy-start.8 = (bf16[512,512]{1,0:T(8,128)(2,1)S(1)}, bf16[512,512]{1,0:T(8,128)(2,1)}, u32[]{:S(2)}) copy-start(bf16[512,512]{1,0:T(8,128)(2,1)} %param.23) | copy-start | bytes 1572868
  101.8 87.8 %copy-start.9 = (bf16[512,512]{1,0:T(8,128)(2,1)S(1)}, bf16[512,512]{1,0:T(8,128)(2,1)}, u32[]{:S(2)}) copy-start(bf16[512,512]{1,0:T(8,128)(2,1)} %param.24) | copy-start | bytes 1572868
  101.8 87.8 %copy-start.10 = (f32[512]{0:T(512)S(1)}, f32[512]{0:T(512)}, u32[]{:S(2)}) copy-start(f32[512]{0:T(512)} %param.25) | copy-start | bytes 6148
  150.8 39.2 %copy-start.2 = (bf16[512,512]{1,0:T(8,128)(2,1)S(1)}, bf16[512,512]{1,0:T(8,128)(2,1)}, u32[]{:S(2)}) copy-start(bf16[512,512]{1,0:T(8,128)(2,1)} %param.26) | copy-start | bytes 1572868
  150.8 39.2 %copy-start.4 = (f32[512]{0:T(512)S(1)}, f32[512]{0:T(512)}, u32[]{:S(2)}) copy-start(f32[512]{0:T(512)} %param.27) | copy-start | bytes 6148
Sparse Core Ops, SparseCore 0:
  8.9 136.6 all-gather.1
